TPU v7x, 128 devices: a whole 4x4x4 slice. The times are simulated.
128 devices in a mesh: row: 8 (over x, core), col: 16 (over z, y).
Axes of the slice: x: 4, y: 4, z: 4, core: 2. Of those that a mesh axis runs over, the one named last changes fastest.
Arguments:
- left_factor: float32 [23, 8, 128, 16, 16, 128], P(None, 'row', None, None, 'col'), may hold values from -5 to 5
- pick_site: int32 [23, 8, 128], P(None, 'row'), may hold values from 0 to 131071
- noise: float32 [23, 8, 128], P(None, 'row'), may hold values from 2 to 5
Outputs:
- panels: float32 [8, 16, 184, 2, 128], P('row', 'col')
All inputs are finite; a program needn't handle non-finite values.
Results may differ from a plain program's by a relative error of at most 0.000064.
Values sent between devices are 32-bit elements; how exact they have to be, the bound alone decides.
No kernel may reach another device: no remote copies, remote signals or barrier semaphores. Data moves between devices by JAX's collectives and lax.ppermute only.
A program may use at most 128 MiB of HBM per device.

v0:
```python
import jax
import jax.numpy as jnp
from jax import lax
from jax.sharding import PartitionSpec as P

GRID_Y = 64
GRID_Z = 32
LATERAL = 24.0
VERTICAL = 6.0


def site_coords(site_ids):
    coord_x = site_ids // (GRID_Y * GRID_Z)
    coord_y = site_ids // GRID_Z % GRID_Y
    coord_z = site_ids % GRID_Z
    return jnp.stack([coord_x, coord_y, coord_z]).astype(jnp.float32)


def matern(row_coords, col_coords):
    lengths = (LATERAL, LATERAL, VERTICAL)
    squared = jnp.zeros((row_coords.shape[1], col_coords.shape[1]), jnp.float32)
    for dim_index in range(3):
        difference = (row_coords[dim_index][:, None] - col_coords[dim_index][None, :]) / lengths[
            dim_index
        ]
        squared = squared + difference * difference
    radius = jnp.sqrt(3.0 * squared)
    return (1.0 + radius) * jnp.exp(-radius)


def times_transposed(left_mat, right_mat):
    return lax.dot_general(
        left_mat,
        right_mat,
        (((1,), (1,)), ((), ())),
        precision=lax.Precision.HIGHEST,
        preferred_element_type=jnp.float32,
    )


def lower_inverse(square):
    factor = jnp.linalg.cholesky(square)
    return jax.scipy.linalg.solve_triangular(
        factor, jnp.eye(square.shape[0], dtype=jnp.float32), lower=True
    )


def body(left_factor, pick_site, noise):
    row_blocks, _, block_width, col_blocks, _, _ = left_factor.shape
    col_count = lax.axis_size("col")
    row_share = row_blocks * block_width // col_count
    row_index = lax.axis_index("row")
    col_index = lax.axis_index("col")
    local_rows = left_factor.reshape(row_blocks * block_width, col_blocks * block_width)
    site_flat = pick_site.reshape(row_blocks * block_width)
    noise_flat = noise.reshape(row_blocks * block_width)
    offset = col_index * row_share
    my_coords = site_coords(lax.dynamic_slice_in_dim(site_flat, offset, row_share))
    my_noise = lax.dynamic_slice_in_dim(noise_flat, offset, row_share)
    first_owner = (row_index == 0) & (col_index == 0)
    second_owner = (row_index == 1) & (col_index == 0)
    own_diag = jnp.diag(my_noise[:block_width])
    head_rows = local_rows[:block_width]
    head_info = jnp.concatenate(
        [site_coords(site_flat[:block_width]), noise_flat[None, :block_width]], axis=0
    )
    is_first = row_index == 0
    is_second = row_index == 1
    heads = jnp.concatenate(
        [jnp.where(is_first, head_rows, 0.0), jnp.where(is_second, head_rows, 0.0)], axis=0
    )
    info = jnp.concatenate(
        [jnp.where(is_first, head_info, 0.0), jnp.where(is_second, head_info, 0.0)], axis=1
    )
    heads, info = lax.psum((heads, info), "row")
    terms = lax.dot_general(
        local_rows.reshape(col_count, row_share, col_blocks * block_width),
        heads,
        (((2,), (1,)), ((), ())),
        precision=lax.Precision.HIGHEST,
        preferred_element_type=jnp.float32,
    )
    gram = lax.psum(times_transposed(heads, heads), "col")
    sums = lax.psum_scatter(terms, "col", scatter_dimension=0, tiled=False)
    first_coords = info[:3, :block_width]
    second_coords = info[:3, block_width:]
    first_diag = matern(first_coords, first_coords) - gram[:block_width, :block_width]
    first_diag = first_diag + jnp.diag(info[3, :block_width])
    first_inverse = lower_inverse(first_diag)
    cross_rows = times_transposed(
        matern(second_coords, first_coords) - gram[block_width:, :block_width], first_inverse
    )
    second_diag = (
        matern(second_coords, second_coords)
        - gram[block_width:, block_width:]
        - times_transposed(cross_rows, cross_rows)
    )
    second_diag = second_diag + jnp.diag(info[3, block_width:])
    second_inverse = lower_inverse(second_diag)
    first_cov = matern(my_coords, first_coords) - sums[:, :block_width]
    first_cov = first_cov.at[:block_width].add(jnp.where(first_owner, own_diag, 0.0))
    first_panel = times_transposed(first_cov, first_inverse)
    second_cov = (
        matern(my_coords, second_coords)
        - sums[:, block_width:]
        - times_transposed(first_panel, cross_rows)
    )
    second_cov = second_cov.at[:block_width].add(jnp.where(second_owner, own_diag, 0.0))
    second_panel = times_transposed(second_cov, second_inverse)
    stacked = jnp.stack([first_panel, second_panel], axis=1)
    return stacked.reshape(1, 1, row_share, 2, block_width)


def solution(mesh):
    placed = (P(None, "row", None, None, "col", None), P(None, "row", None), P(None, "row", None))
    return jax.shard_map(
        body,
        mesh=mesh,
        in_specs=placed,
        out_specs=P("row", "col", None, None, None),
        check_vma=False,
    )
```

profile of v0, /device:TPU:0, one launch (start us, length us, event | category | flops | bytes accessed | tf_op | source)
XLA Modules:
  0.0 291.8 jit_solution(3037362575774388247)
XLA Ops:
  6.5 6.9 %fusion.6 = (f32[128,16,128]{2,1,0:T(8,128)S(1)}, f32[128,16,128]{2,1,0:T(8,128)S(1)}) fusion(pred[]{:T(512)S(6)} %eq.34, f32[23,1,128,16,1,128]{5,4,3,2,1,0:T(1,128)} %param.10, pred[]{:T(512)S(6)} %eq.35), kind=kLoop, calls=%fused_computation.10 | loop fusion | flops 524288 | bytes 3145730 | tf_op jit(solution)/shard_map/jit(_where)/select_n | solution.py:70
  13.5 0.9 copy_bitcast_fusion
  14.3 1.5 pad_maximum_fusion
  15.9 0.5 broadcast.389
  16.4 66.7 %reduce.21 = f32[23,128,16,128]{3,2,1,0:T(8,128)} reduce(f32[23,1,128,16,1,128]{5,4,3,2,1,0:T(1,128)} %param.10, f32[]{:T(128)} %broadcast.389), dimensions={1,4}, to_apply=%param.10.reduce_sub_computation.3 | reduce | bytes 48234500 | tf_op args[0]
  83.1 26.4 %reshape_reshape.3 = f32[16,184,2048]{2,1,0:T(8,128)} reshape(f32[23,128,16,128]{3,2,1,0:T(8,128)} %reduce.21) | data formatting | bytes 48234496 | tf_op jit(solution)/shard_map/reshape;reshape | solution.py:77
  109.5 4.9 %fusion.60 = f32[256,256]{0,1:T(8,128)} fusion(f32[256,2048]{1,0:T(8,128)} %all-reduce.4.cloned.1.call-done), kind=kOutput, calls=%fused_computation.128 | convolution fusion | flops 1610612736 | bytes 2359296 | tf_op jit(solution)/shard_map/dot_general | solution.py:32
  114.5 0.2 reduce-scatter.4.cloned.1.call-start
  114.7 23.1 %fusion.2 = f32[16,184,256]{2,1,0:T(8,128)} fusion(f32[16,184,2048]{2,1,0:T(8,128)} %reshape_reshape.3, f32[256,2048]{1,0:T(8,128)S(1)} %copy-done), kind=kOutput, calls=%fused_computation.5 | convolution fusion | flops 18522046464 | bytes 29229056 | tf_op jit(solution)/shard_map/dot_general | solution.py:76
  137.8 0.7 copy-done.1
  138.8 14.7 %psum.21 = f32[4,256]{1,0:T(4,128)S(1)} all-reduce(f32[4,256]{1,0:T(4,128)S(1)} %pad_maximum_fusion.1), channel_id=1, replica_groups=mesh['row'=8,'col'=16] {'row'}, use_global_device_ids=true, to_apply=%region_0.1 | all-reduce | flops 1024 | bytes 8192 | tf_op jit(solution)/shard_map/psum | solution.py:75
  153.6 48.5 %all-reduce.6.cloned.1.call-done = f32[256,256]{0,1:T(8,128)} async-done(((f32[256,256]{0,1:T(8,128)}), f32[256,256]{0,1:T(8,128)}) %all-reduce.6.cloned.1.call-update) | async-done | bytes 262160 | tf_op jit(solution)/shard_map/psum | solution.py:83
  202.2 1.0 fusion.19
  203.3 1.0 fusion.23
  204.3 11.7 %cholesky.44 = f32[128,128]{1,0:T(8,128)S(1)} custom-call(f32[128,128]{1,0:T(8,128)S(1)} %fusion.23), custom_call_target="Cholesky" | custom-call | tf_op jit(solution)/shard_map/jit(cholesky)/cholesky | solution.py:42
  216.0 0.6 compare_reduce_fusion.1
  216.7 0.7 fusion.12
  217.3 9.8 %custom-call.6 = f32[1,128,128]{1,2,0:T(8,128)S(1)} custom-call(f32[1,128,128]{2,1,0:T(8,128)S(1)} %fusion.12), custom_call_target="InvertDiagBlocksLowerTriangular" | custom-call | tf_op jit(solution)/shard_map/jit(_solve_triangular)/triangular_solve | solution.py:43
  227.1 0.3 fusion.10
  227.4 1.2 fusion.18
  228.7 1.1 fusion.5
  229.9 11.7 %cholesky.55 = f32[128,128]{1,0:T(8,128)S(1)} custom-call(f32[128,128]{1,0:T(8,128)S(1)} %fusion.21), custom_call_target="Cholesky" | custom-call | tf_op jit(solution)/shard_map/jit(cholesky)/cholesky | solution.py:42
  241.7 0.6 compare_reduce_fusion
  242.3 0.7 fusion.13
  243.0 10.0 %custom-call.7 = f32[1,128,128]{1,2,0:T(8,128)S(1)} custom-call(f32[1,128,128]{2,1,0:T(8,128)S(1)} %fusion.13), custom_call_target="InvertDiagBlocksLowerTriangular" | custom-call | tf_op jit(solution)/shard_map/jit(_solve_triangular)/triangular_solve | solution.py:43
  253.0 0.3 fusion.8
  253.3 28.7 %reduce-scatter.4.cloned.1.call-done = f32[1,184,256]{2,1,0:T(8,128)} async-done(((f32[16,184,256]{2,1,0:T(8,128)}), f32[1,184,256]{2,1,0:T(8,128)}) %reduce-scatter.4.cloned.1.call-update) | async-done | bytes 188432
  281.9 1.1 copy.19
  283.2 0.4 fusion.61
  283.6 0.4 convolution_subtract_fusion
  284.0 0.4 convolution_bitcast_fusion
  284.5 0.8 copy.26
  (33 shorter events, 0.9 us)
Async XLA Ops:
  6.5 103.0 %all-reduce.4.cloned.1.call-start = ((), (), s32[]{:S(2)}) async-start(), calls=%async_computation.1 | async-start | bytes 4194304 | tf_op jit(solution)/shard_map/psum | solution.py:75
  15.8 186.3 %all-reduce.6.cloned.1.call-start = ((), (), s32[]{:S(2)}) async-start(), calls=%async_computation.2 | async-start | bytes 524288 | tf_op jit(solution)/shard_map/psum | solution.py:83
  109.5 5.2 %copy-start = (f32[256,2048]{1,0:T(8,128)S(1)}, f32[256,2048]{1,0:T(8,128)}, u32[]{:S(2)}) copy-start(f32[256,2048]{1,0:T(8,128)} %all-reduce.4.cloned.1.call-done) | copy-start | bytes 6291460
  114.5 167.5 %reduce-scatter.4.cloned.1.call-start = ((), (), s32[]{:S(2)}) async-start(), calls=%async_computation.3 | async-start | bytes 3203072
  137.8 0.7 copy-start.1
  137.8 0.7 copy-start.2
Sparse Core Ops, SparseCore 0:
  15.9 68.0 all-reduce.3
  114.6 87.5 all-reduce.5
  205.5 76.3 reduce-scatter.3
where the time goes:
time: 293 us; the launch traced here: 292 us
  other arithmetic  123 us (42%)
  waiting for transfers between devices  77.3 us (26%)
  matrix products  32.1 us (11%)
  local copies, waits for them, and re-layouts  30.6 us (10%)
  blocking collectives  14.7 us (5%)
  between operations  13.4 us (5%)
    unnamed x3, other arithmetic  66.7 us
    psum x1, waiting for transfers between devices, body(): gram = lax.psum(times_transposed(heads, heads), 'col')  48.5 us
    unnamed x4, waiting for transfers between devices  28.7 us
    another operation x1, local copies, waits for them, and re-layouts, body(): local_rows.reshape(col_count, row_share, col_blocks * block_width)  26.4 us
    another operation x6, other arithmetic, lower_inverse(): factor = jnp.linalg.cholesky(square)  24.8 us
    dot_general x1, matrix products, body(): lax.dot_general(local_rows.reshape(col_count, row_share, col_blocks * blo...  23.1 us
    another operation x4, other arithmetic, lower_inverse(): jax.scipy.linalg.solve_triangular(factor, jnp.eye(square.shape[0], dtype=...  21.1 us
    psum x1, blocking collectives, body(): heads, info = lax.psum((heads, info), 'row')  14.7 us
  transfers between devices with their start and end apart: 3, of which 2 were waited for; matrix products, arithmetic and copies ran while one was open for 58% of the time, Pallas kernels for 0%

commit v1 on v0

--- a/solution.py
+++ b/solution.py
@@ -80,7 +80,7 @@
         precision=lax.Precision.HIGHEST,
         preferred_element_type=jnp.float32,
     )
-    gram = lax.psum(times_transposed(heads, heads), "col")
+    gram = jnp.sum(lax.all_gather(times_transposed(heads, heads), "col"), axis=0)
     sums = lax.psum_scatter(terms, "col", scatter_dimension=0, tiled=False)
     first_coords = info[:3, :block_width]
     second_coords = info[:3, block_width:]

time: 293 us -> 326 us (1.11)
  waiting for transfers between devices: 77.3 us -> 111 us
  matrix products: 32.1 us -> 28.7 us
    all_gather x0 -> x1, waiting for transfers between devices: none -> 51.6 us  [body(): lax.all_gather(times_transposed(heads, heads), 'col')]
    psum x1 -> x0, waiting for transfers between devices: 48.5 us -> none  [body(): gram = lax.psum(times_transposed(heads, heads), 'col')]
    unnamed x4, waiting for transfers between devices: 28.7 us -> 59.4 us
    dot_general x6, matrix products: 8.48 us -> 4.42 us  [times_transposed(): lax.dot_general(left_mat, right_mat, (((1,), (1,)), ((), ())), precision=...]
  transfers between devices with their start and end apart: 3 -> 3, of which waited for: 2 -> 2; matrix products, arithmetic and copies ran while one was open for 58% -> 30% of each run, Pallas kernels for 0% -> 0%
where the time goes in v1:
time: 326 us; the launch traced here: 325 us
  other arithmetic  124 us (38%)
  waiting for transfers between devices  111 us (34%)
  local copies, waits for them, and re-layouts  31.7 us (10%)
  matrix products  28.7 us (9%)
  blocking collectives  15.3 us (5%)
  between operations  13.4 us (4%)
    unnamed x3, other arithmetic  66.8 us
    unnamed x4, waiting for transfers between devices  59.4 us
    all_gather x1, waiting for transfers between devices, body(): lax.all_gather(times_transposed(heads, heads), 'col')  51.6 us
    another operation x1, local copies, waits for them, and re-layouts, body(): local_rows.reshape(col_count, row_share, col_blocks * block_width)  26.4 us
    another operation x6, other arithmetic, lower_inverse(): factor = jnp.linalg.cholesky(square)  25 us
    dot_general x1, matrix products, body(): lax.dot_general(local_rows.reshape(col_count, row_share, col_blocks * blo...  23.7 us
    another operation x4, other arithmetic, lower_inverse(): jax.scipy.linalg.solve_triangular(factor, jnp.eye(square.shape[0], dtype=...  20.9 us
    psum x1, blocking collectives, body(): heads, info = lax.psum((heads, info), 'row')  15.3 us
  transfers between devices with their start and end apart: 3, of which 2 were waited for; matrix products, arithmetic and copies ran while one was open for 30% of the time, Pallas kernels for 0%

profile of v1, /device:TPU:0, one launch (start us, length us, event | category | flops | bytes accessed | tf_op | source)
XLA Modules:
  0.0 324.6 jit_solution(7010772381882553838)
XLA Ops:
  6.5 6.9 %fusion.6 = (f32[128,16,128]{2,1,0:T(8,128)S(1)}, f32[128,16,128]{2,1,0:T(8,128)S(1)}) fusion(pred[]{:T(512)S(6)} %eq.34, f32[23,1,128,16,1,128]{5,4,3,2,1,0:T(1,128)} %param.10, pred[]{:T(512)S(6)} %eq.35), kind=kLoop, calls=%fused_computation.10 | loop fusion | flops 524288 | bytes 3145730 | tf_op jit(solution)/shard_map/jit(_where)/select_n | solution.py:70
  13.5 0.9 copy_bitcast_fusion
  14.3 1.5 pad_maximum_fusion
  15.8 0.2 reduce-scatter.4.cloned.1.call-start
  16.1 0.5 broadcast.389
  16.6 66.7 %reduce.21 = f32[23,128,16,128]{3,2,1,0:T(8,128)} reduce(f32[23,1,128,16,1,128]{5,4,3,2,1,0:T(1,128)} %param.10, f32[]{:T(128)} %broadcast.389), dimensions={1,4}, to_apply=%param.10.reduce_sub_computation.3 | reduce | bytes 48234500 | tf_op args[0]
  83.3 26.4 %reshape_reshape.3 = f32[16,184,2048]{2,1,0:T(8,128)} reshape(f32[23,128,16,128]{3,2,1,0:T(8,128)} %reduce.21) | data formatting | bytes 48234496 | tf_op jit(solution)/shard_map/reshape;reshape | solution.py:77
  109.7 23.7 %fusion.2 = f32[16,184,256]{2,1,0:T(8,128)} fusion(f32[16,184,2048]{2,1,0:T(8,128)} %reshape_reshape.3, f32[256,2048]{1,0:T(8,128)} %all-reduce.3.cloned.1.call-done), kind=kOutput, calls=%fused_computation.5 | convolution fusion | flops 18522046464 | bytes 29229056 | tf_op jit(solution)/shard_map/dot_general | solution.py:76
  133.5 1.5 copy-done
  135.0 2.6 fusion.61
  137.9 15.3 %psum.14 = f32[4,256]{1,0:T(4,128)S(1)} all-reduce(f32[4,256]{1,0:T(4,128)S(1)} %pad_maximum_fusion.1), channel_id=1, replica_groups=mesh['row'=8,'col'=16] {'row'}, use_global_device_ids=true, to_apply=%region_0.1 | all-reduce | flops 1024 | bytes 8192 | tf_op jit(solution)/shard_map/psum | solution.py:75
  153.3 59.3 %reduce-scatter.4.cloned.1.call-done = f32[1,184,256]{2,1,0:T(8,128)} async-done(((f32[16,184,256]{2,1,0:T(8,128)}), f32[1,184,256]{2,1,0:T(8,128)}) %reduce-scatter.4.cloned.1.call-update) | async-done | bytes 188432
  212.7 1.1 copy.20
  213.7 0.2 slice_subtract_fusion.1
  214.0 51.6 %all-gather.3.cloned.1.call-done = f32[4096,256]{1,0:T(8,128)} async-done(((f32[256,256]{1,0:T(8,128)}), f32[4096,256]{1,0:T(8,128)}) %all-gather.3.cloned.1.call-update) | async-done | bytes 4194320 | tf_op jit(solution)/shard_map/all_gather | solution.py:83
  265.5 2.5 reduce_sum.9
  268.5 11.7 %cholesky.44 = f32[128,128]{1,0:T(8,128)S(1)} custom-call(f32[128,128]{1,0:T(8,128)S(1)} %fusion.21), custom_call_target="Cholesky" | custom-call | tf_op jit(solution)/shard_map/jit(cholesky)/cholesky | solution.py:42
  280.3 0.6 compare_reduce_fusion.1
  280.9 0.7 fusion.12
  281.6 9.8 %custom-call.6 = f32[1,128,128]{1,2,0:T(8,128)S(1)} custom-call(f32[1,128,128]{2,1,0:T(8,128)S(1)} %fusion.12), custom_call_target="InvertDiagBlocksLowerTriangular" | custom-call | tf_op jit(solution)/shard_map/jit(_solve_triangular)/triangular_solve | solution.py:43
  291.4 0.3 fusion.10
  291.9 0.4 fusion.62
  292.3 0.4 fusion.22
  292.7 0.4 convolution_subtract_fusion
  293.1 0.3 fusion.5
  293.5 11.9 %cholesky.55 = f32[128,128]{1,0:T(8,128)S(1)} custom-call(f32[128,128]{1,0:T(8,128)S(1)} %fusion.19), custom_call_target="Cholesky" | custom-call | tf_op jit(solution)/shard_map/jit(cholesky)/cholesky | solution.py:42
  305.4 0.6 compare_reduce_fusion
  306.1 0.7 fusion.13
  306.7 9.8 %custom-call.7 = f32[1,128,128]{1,2,0:T(8,128)S(1)} custom-call(f32[1,128,128]{2,1,0:T(8,128)S(1)} %fusion.13), custom_call_target="InvertDiagBlocksLowerTriangular" | custom-call | tf_op jit(solution)/shard_map/jit(_solve_triangular)/triangular_solve | solution.py:43
  316.5 0.3 fusion.8
  316.9 0.4 convolution_bitcast_fusion
  317.3 0.8 copy.29
  (38 shorter events, 1.4 us)
Async XLA Ops:
  6.5 103.1 %all-reduce.3.cloned.1.call-start = ((), (), s32[]{:S(2)}) async-start(), calls=%async_computation.1 | async-start | bytes 4194304 | tf_op jit(solution)/shard_map/psum | solution.py:75
  15.8 196.8 %reduce-scatter.4.cloned.1.call-start = ((), (), s32[]{:S(2)}) async-start(), calls=%async_computation.3 | async-start | bytes 3203072
  133.4 1.6 copy-start
  133.4 4.2 %copy-start.1 = (s32[23,1,128]{2,1,0:T(1,128)S(1)}, s32[23,1,128]{2,1,0:T(1,128)}, u32[]{:S(2)}) copy-start(s32[23,1,128]{2,1,0:T(1,128)} %param.11) | copy-start | bytes 35332
  133.4 4.2 %copy-start.2 = (f32[23,1,128]{2,1,0:T(1,128)S(1)}, f32[23,1,128]{2,1,0:T(1,128)}, u32[]{:S(2)}) copy-start(f32[23,1,128]{2,1,0:T(1,128)} %param.12) | copy-start | bytes 35332
  133.5 132.1 %all-gather.3.cloned.1.call-start = ((), (), s32[]{:S(2)}) async-start(), calls=%async_computation.2 | async-start | bytes 4456448 | tf_op jit(solution)/shard_map/all_gather | solution.py:83
Sparse Core Ops, SparseCore 0:
  15.9 68.0 all-reduce.2
  133.6 79.0 reduce-scatter.3
  214.8 50.6 all-gather.2
